TPU v7x, 512 devices: a whole 4x8x8 slice. The times are simulated.
512 devices in a mesh: shard: 128 (over y, z, core), tensor: 4 (over x).
Axes of the slice: x: 4, y: 8, z: 8, core: 2. Of those that a mesh axis runs over, the one named last changes fastest.
Arguments:
- big_grad: bfloat16 [32, 1280, 768], P(None, 'shard', 'tensor')
- big_weight: bfloat16 [32, 1280, 768], P(None, 'shard', 'tensor'), may hold values from -0.017944336 to 0.017944336
- big_moment: float32 [128, 768, 1280], P('shard', 'tensor'), may hold values from -6 to 6
- small_grad: bfloat16 [32, 1280, 192], P(None, 'shard')
- small_weight: bfloat16 [32, 1280, 192], P(None, 'shard'), may hold values from -0.15625 to 0.15625
- small_moment: float32 [128, 192, 1280], P('shard'), may hold values from -6 to 6
- owners: int32 [2, 32], replicated, may hold values from 0 to 127, as said below
- vec_parts: float32 [128, 43008], P('shard'), may hold values from -0.6 to 0.6
- vec_param: float32 [43008], P('shard'), may hold values from 0.5 to 1.5
- vec_first: float32 [43008], P('shard'), may hold values from -0.6 to 0.6
- vec_second: float32 [43008], P('shard'), may hold values from 0.01 to 1
Outputs:
- big_weight_new: bfloat16 [32, 1280, 768], P(None, 'shard', 'tensor')
- big_moment_new: float32 [128, 768, 1280], P('shard', 'tensor')
- small_weight_new: bfloat16 [32, 1280, 192], P(None, 'shard')
- small_moment_new: float32 [128, 192, 1280], P('shard')
- vec_param_new: float32 [43008], P('shard')
- vec_first_new: float32 [43008], P('shard')
- vec_second_new: float32 [43008], P('shard')
Inputs may be any that keep to these rules, and one draw needn't show every extreme that they name: `owners`: no shard index appears twice in the whole list (over both rows); each aligned group of four shard indices holds exactly one owner of each row; the first and the last shard index own a matrix.
All inputs are finite; a program needn't handle non-finite values.
Results may differ from a plain program's by a relative error of at most 0.0068.
Values may be sent and summed in bfloat16 or wider, within the bound.
No kernel may reach another device: no remote copies, remote signals or barrier semaphores. Data moves between devices by JAX's collectives and lax.ppermute only.
A program may use at most 64 MiB of HBM per device.

v0:
```python
import math
import jax
import jax.numpy as jnp
from jax import lax
from jax.sharding import PartitionSpec as P

D = 1280
ITERS = 2
newton_linear = 3.4445
newton_cubic = -4.775
newton_quintic = 2.0315
momentum_rate = 0.95
muon_rate = 0.05
weight_decay = 0.1
norm_epsilon = 1e-07
adam_rate = 0.004
first_decay = 0.9
second_decay = 0.95
adam_epsilon = 1e-08
first_correct = 0.99997343860111
second_correct = 0.99407947077967


def owner_table(owner_list, count):
    devices = lax.broadcasted_iota(jnp.int32, (count, owner_list.shape[0]), 0)
    return (devices == owner_list[None, :]).astype(jnp.bfloat16)


def route_rows(owner_map, pieces):
    flattened = pieces.reshape(pieces.shape[0], -1)
    routed = jnp.dot(owner_map, flattened, preferred_element_type=jnp.float32)
    return routed.astype(jnp.bfloat16).reshape((owner_map.shape[0],) + pieces.shape[1:])


def collect(owner_map, arrived):
    flattened = arrived.reshape(arrived.shape[0], -1)
    picked = lax.dot_general(
        owner_map, flattened, (((0,), (0,)), ((), ())), preferred_element_type=jnp.float32
    )
    return picked.astype(jnp.bfloat16).reshape((owner_map.shape[1],) + arrived.shape[1:])


def advance(arrived, moment, is_owner):
    gradient = arrived.T.astype(jnp.float32)
    renewed = momentum_rate * moment + gradient
    retained = jnp.where(is_owner, renewed, moment)
    blended = jnp.where(is_owner, gradient + momentum_rate * renewed, 0.0).astype(jnp.bfloat16).T
    return (retained, blended)


def normalized(field):
    values = field.astype(jnp.float32)
    squares = jnp.sum(values * values)
    return (values / (jnp.sqrt(squares) + norm_epsilon)).astype(jnp.bfloat16)


def gram_block(left_part, right_part):
    product = lax.dot_general(
        left_part, right_part, (((0,), (0,)), ((), ())), preferred_element_type=jnp.float32
    )
    return product.astype(jnp.bfloat16)


def poly_block(gram_part, gram_full):
    square = jnp.dot(gram_part, gram_full, preferred_element_type=jnp.float32)
    return (newton_cubic * gram_part.astype(jnp.float32) + newton_quintic * square).astype(
        jnp.bfloat16
    )


def newton_step(column_part, full_iterate, polynomial):
    product = lax.dot_general(
        full_iterate, polynomial, (((1,), (1,)), ((), ())), preferred_element_type=jnp.float32
    )
    return (newton_linear * column_part.astype(jnp.float32) + product).astype(jnp.bfloat16)


def small_newton(field):
    iterate = normalized(field)
    for iteration in range(ITERS):
        gram_full = gram_block(iterate, iterate)
        iterate = newton_step(iterate, iterate, poly_block(gram_full, gram_full))
    return iterate


def apply_update(weight, update):
    scale = 0.2 * math.sqrt(D)
    values = weight.astype(jnp.float32)
    return (
        values - muon_rate * (scale * update.astype(jnp.float32) + weight_decay * values)
    ).astype(jnp.bfloat16)


def gather_columns(column_part):
    return lax.all_gather(column_part, "tensor", axis=1, tiled=True)


def gather_gram(gram_part):
    return lax.all_gather(gram_part, "tensor", axis=0, tiled=True)


def per_device(
    big_grad,
    big_weight,
    big_moment,
    small_grad,
    small_weight,
    small_moment,
    owners,
    vec_parts,
    vec_param,
    vec_first,
    vec_second,
):
    shards = lax.axis_size("shard")
    shard_place = lax.axis_index("shard")
    column = lax.axis_index("tensor")
    block_width = big_grad.shape[2]
    rows_dev = big_grad.shape[1]
    matrices = big_grad.shape[0]
    joint_map = owner_table(jnp.concatenate([owners[0], owners[1]]), shards)
    joint_pieces = jnp.concatenate([big_grad, small_grad], axis=0)
    arrived = lax.all_to_all(
        route_rows(joint_map, joint_pieces), "shard", split_axis=0, concat_axis=1, tiled=True
    )[0]
    big_owner = jnp.any(owners[0] == shard_place)
    small_owner = jnp.any(owners[1] == shard_place)
    big_retained, big_blended = advance(arrived, big_moment[0], big_owner)
    small_retained, small_blended = advance(arrived, small_moment[0], small_owner)
    small_result = small_newton(small_blended)
    full_iterate = normalized(gather_columns(big_blended))
    for iteration in range(ITERS - 1):
        gram_full = gram_block(full_iterate, full_iterate)
        full_iterate = newton_step(full_iterate, full_iterate, poly_block(gram_full, gram_full))
    gram_full = gram_block(full_iterate, full_iterate)
    gram_rows = lax.dynamic_slice_in_dim(gram_full, column * block_width, block_width, 0)
    owned_part = lax.dynamic_slice_in_dim(full_iterate, column * block_width, block_width, 1)
    big_result = newton_step(owned_part, full_iterate, poly_block(gram_rows, gram_full))
    own_result = jnp.where(big_owner, big_result, small_result)
    returned = lax.all_to_all(
        own_result.reshape(shards, rows_dev, block_width),
        "shard",
        split_axis=0,
        concat_axis=0,
        tiled=True,
    )
    picked = collect(joint_map, returned)
    big_weight_new = apply_update(big_weight, picked[:matrices])
    small_weight_new = apply_update(small_weight, picked[matrices:])
    vec_pieces = vec_parts[0].reshape(shards, -1)
    grad_share = jnp.sum(
        lax.all_to_all(vec_pieces, "shard", split_axis=0, concat_axis=0, tiled=True), axis=0
    )
    first_new = first_decay * vec_first + (1.0 - first_decay) * grad_share
    second_new = second_decay * vec_second + (1.0 - second_decay) * grad_share * grad_share
    param_new = vec_param - adam_rate * (first_new / first_correct) / (
        jnp.sqrt(second_new / second_correct) + adam_epsilon
    )
    return (
        big_weight_new,
        big_retained[None],
        small_weight_new,
        small_retained[None],
        param_new,
        first_new,
        second_new,
    )


def solution(mesh):
    return jax.shard_map(
        per_device,
        mesh=mesh,
        in_specs=(
            P(None, "shard", "tensor"),
            P(None, "shard", "tensor"),
            P("shard", "tensor", None),
            P(None, "shard", None),
            P(None, "shard", None),
            P("shard", None, None),
            P(),
            P("shard", None),
            P("shard"),
            P("shard"),
            P("shard"),
        ),
        out_specs=(
            P(None, "shard", "tensor"),
            P("shard", "tensor", None),
            P(None, "shard", None),
            P("shard", None, None),
            P("shard"),
            P("shard"),
            P("shard"),
        ),
        check_vma=False,
    )
```

profile of v0, /device:TPU:1, one launch (start us, length us, event | category | flops | bytes accessed | tf_op | source)
XLA Modules:
  0.0 153.9 jit_solution(12986507688042528019)
XLA Ops:
  7.2 0.8 slice_bitcast_fusion.1
  7.9 1.0 pad_maximum_fusion
  9.0 0.2 copy.32
  9.2 0.4 reshape.45
  9.6 0.1 pad_add_fusion
  9.6 0.3 convolution_convert_fusion
  9.9 0.3 copy.33
  10.2 1.3 copy.34
  11.5 1.6 %reshape.59 = bf16[128,2,960]{2,1,0:T(2,128)(2,1)} reshape(bf16[128,10,192]{2,1,0:T(8,128)(2,1)S(1)} %copy.34) | data formatting | bytes 983040
  13.1 18.4 %all-to-all-start = ((bf16[128,2,960]{2,1,0:T(2,128)(2,1)}), bf16[128,2,960]{2,1,0:T(2,128)(2,1)S(1)}, u32[]{:S(2)}, u32[]{:S(2)}) async-start(bf16[128,2,960]{2,1,0:T(2,128)(2,1)} %reshape.59), calls=%async_computation | async-start | bytes 1048576 | tf_op jit(solution)/shard_map/all_to_all | solution.py:123
  31.5 0.0 all-gather.2.cloned.1.call-start
  31.6 0.6 compare_reduce_fusion.1
  32.2 18.7 %all-to-all-done = bf16[128,2,960]{2,1,0:T(2,128)(2,1)S(1)} async-done(((bf16[128,2,960]{2,1,0:T(2,128)(2,1)}), bf16[128,2,960]{2,1,0:T(2,128)(2,1)S(1)}, u32[]{:S(2)}, u32[]{:S(2)}) %all-to-all-start) | async-done | bytes 491552 | tf_op jit(solution)/shard_map/all_to_all | solution.py:123
  50.9 0.8 reshape.60
  51.7 0.4 reshape.49
  52.1 0.4 copy.35
  52.5 0.8 copy-done.1
  53.3 4.9 %fusion.17 = (f32[1,192,1280]{2,1,0:T(8,128)}, bf16[1280,192]{0,1:T(8,128)(2,1)}, f32[1,192,1280]{2,1,0:T(8,128)}, f32[]{:T(128)}, bf16[192,1280]{1,0:T(8,128)(2,1)S(1)}) fusion(f32[1,192,1280]{2,1,0:T(8,128)S(1)} %copy-done.1, f32[1280,192]{0,1:T(8,128)S(1)} %copy.35, pred[]{:T(512)} %get-tuple-element.21, f32[1,192,1280]{2,1,0:T(8,128)} %param.16, ...), kind=kLoop, calls=%fused_computation.39 | loop fusion | flops 4177919 | bytes 5898246 | tf_op jit(solution)/shard_map/broadcast_in_dim | solution.py:161
  58.2 0.5 broadcast.71
  58.7 1.0 reduce.5
  59.8 1.0 all_to_all.20
  60.8 7.3 %all-to-all-start.2 = ((f32[128,1,336]{2,1,0:T(1,128)}), f32[128,1,336]{2,1,0:T(1,128)S(1)}, u32[]{:S(2)}, u32[]{:S(2)}) async-start(f32[128,1,336]{2,1,0:T(1,128)} %all_to_all.20), calls=%async_computation.2 | async-start | bytes 393216 | tf_op jit(solution)/shard_map/all_to_all | solution.py:152
  68.7 0.3 convolution_convert_fusion.5
  69.1 0.4 fusion.3
  69.5 0.3 convolution_convert_fusion.4
  69.8 0.4 fusion.4
  70.3 16.5 %all-gather.2.cloned.1.call-done = bf16[1280,768]{0,1:T(8,128)(2,1)} async-done(((bf16[1280,192]{0,1:T(8,128)(2,1)}), bf16[1280,768]{0,1:T(8,128)(2,1)}) %all-gather.2.cloned.1.call-update) | async-done | bytes 1966096 | tf_op jit(solution)/shard_map/all_gather | solution.py:95
  86.8 3.3 %fusion = f32[]{:T(128)} fusion(bf16[1280,768]{0,1:T(8,128)(2,1)} %all-gather.2.cloned.1.call-done), kind=kLoop, calls=%fused_computation.2 | loop fusion | flops 2949119 | bytes 1966084 | tf_op jit(solution)/shard_map/reduce_sum | solution.py:53
  90.8 2.8 %convolution_convert_fusion.3 = bf16[768,768]{1,0:T(8,128)(2,1)} fusion(bf16[1280,768]{0,1:T(8,128)(2,1)S(1)} %copy-done, f32[]{:T(128)S(6)} %add.66), kind=kOutput, calls=%fused_computation.16 | convolution fusion | flops 1513488384 | bytes 3145732 | tf_op jit(solution)/shard_map/dot_general | solution.py:58
  93.6 6.3 %add_convert_fusion = bf16[1280,768]{0,1:T(8,128)(2,1)} fusion(bf16[768,768]{1,0:T(8,128)(2,1)} %convolution_convert_fusion.3, f32[]{:T(128)S(6)} %add.66, bf16[1280,768]{0,1:T(8,128)(2,1)S(1)} %copy-done), kind=kOutput, calls=%fused_computation.4 | convolution fusion | flops 2428698624 | bytes 5111812 | tf_op jit(solution)/shard_map/dot_general | solution.py:72
  99.9 3.8 %convolution_convert_fusion.2 = bf16[768,768]{1,0:T(8,128)(2,1)S(1)} fusion(bf16[1280,768]{0,1:T(8,128)(2,1)} %add_convert_fusion), kind=kOutput, calls=%fused_computation.15 | convolution fusion | flops 1510539264 | bytes 3145728 | tf_op jit(solution)/shard_map/dot_general | solution.py:58
  103.7 3.2 %fusion.5 = bf16[1280,192]{0,1:T(8,128)(2,1)S(1)} fusion(bf16[1280,192]{0,1:T(8,128)(2,1)S(1)} %fusion.4, bf16[1280,768]{0,1:T(8,128)(2,1)} %add_convert_fusion, bf16[768,768]{1,0:T(8,128)(2,1)S(1)} %convolution_convert_fusion.2, s32[]{:T(128)S(6)} %select_n.39, pred[]{:T(512)} %get-tuple-element.21), kind=kOutput, calls=%fused_computation.11 | convolution fusion | flops 605945856 | bytes 5212160 | tf_op jit(solution)/shard_map/dot_general | solution.py:72
  106.9 0.2 copy.36
  107.2 0.3 reshape.47
  107.5 1.6 %reshape.61 = bf16[128,2,960]{2,1,0:T(2,128)(2,1)} reshape(bf16[128,10,192]{2,1,0:T(8,128)(2,1)S(1)} %reshape.47) | data formatting | bytes 983040
  109.1 14.5 %all-to-all-start.1 = ((bf16[128,2,960]{2,1,0:T(2,128)(2,1)}), bf16[128,2,960]{2,1,0:T(2,128)(2,1)S(1)}, u32[]{:S(2)}, u32[]{:S(2)}) async-start(bf16[128,2,960]{2,1,0:T(2,128)(2,1)} %reshape.61), calls=%async_computation.1 | async-start | bytes 1048576 | tf_op jit(solution)/shard_map/all_to_all | solution.py:140
  123.5 0.2 reduce_sum.29
  123.7 0.6 divide_subtract_fusion
  124.3 18.6 %all-to-all-done.1 = bf16[128,2,960]{2,1,0:T(2,128)(2,1)S(1)} async-done(((bf16[128,2,960]{2,1,0:T(2,128)(2,1)}), bf16[128,2,960]{2,1,0:T(2,128)(2,1)S(1)}, u32[]{:S(2)}, u32[]{:S(2)}) %all-to-all-start.1) | async-done | bytes 491552 | tf_op jit(solution)/shard_map/all_to_all | solution.py:140
  143.0 0.8 reshape.62
  143.7 0.7 copy.37
  144.5 0.3 convolution_convert_fusion.1
  144.9 0.2 mul.156
  145.0 0.2 fusion.26
  145.2 0.7 copy.40
  145.9 0.2 mul.160
  146.1 0.2 fusion.29
  146.3 0.7 copy.41
  (20 shorter events, 0.1 us)
Async XLA Ops:
  10.2 21.4 %copy-start.5 = (s32[2,32]{1,0:T(2,128)S(1)}, s32[2,32]{1,0:T(2,128)}, u32[]{:S(2)}) copy-start(s32[2,32]{1,0:T(2,128)} %param.17) | copy-start | bytes 772
  13.1 37.8 %all-to-all-start = ((bf16[128,2,960]{2,1,0:T(2,128)(2,1)}), bf16[128,2,960]{2,1,0:T(2,128)(2,1)S(1)}, u32[]{:S(2)}, u32[]{:S(2)}) async-start(bf16[128,2,960]{2,1,0:T(2,128)(2,1)} %reshape.59), calls=%async_computation | async-start | bytes 1048576 | tf_op jit(solution)/shard_map/all_to_all | solution.py:123
  31.5 55.3 %all-gather.2.cloned.1.call-start = ((), (), s32[]{:S(2)}) async-start(), calls=%async_computation.3 | async-start | bytes 2457600 | tf_op jit(solution)/shard_map/all_gather | solution.py:95
  52.1 1.2 copy-start.1
  53.3 5.4 %copy-start.2 = (f32[1,43008]{1,0:T(1,128)S(1)}, f32[1,43008]{1,0:T(1,128)}, u32[]{:S(2)}) copy-start(f32[1,43008]{1,0:T(1,128)} %param.18) | copy-start | bytes 516100
  60.8 48.3 %all-to-all-start.2 = ((f32[128,1,336]{2,1,0:T(1,128)}), f32[128,1,336]{2,1,0:T(1,128)S(1)}, u32[]{:S(2)}, u32[]{:S(2)}) async-start(f32[128,1,336]{2,1,0:T(1,128)} %all_to_all.20), calls=%async_computation.2 | async-start | bytes 393216 | tf_op jit(solution)/shard_map/all_to_all | solution.py:152
  86.8 4.0 %copy-start = (bf16[1280,768]{0,1:T(8,128)(2,1)S(1)}, bf16[1280,768]{0,1:T(8,128)(2,1)}, u32[]{:S(2)}) copy-start(bf16[1280,768]{0,1:T(8,128)(2,1)} %all-gather.2.cloned.1.call-done) | copy-start | bytes 5898244
  107.2 16.5 %copy-start.6 = (f32[336]{0:T(512)S(1)}, f32[336]{0:T(512)}, u32[]{:S(2)}) copy-start(f32[336]{0:T(512)} %param.19) | copy-start | bytes 4036
  107.2 16.5 %copy-start.7 = (f32[336]{0:T(512)S(1)}, f32[336]{0:T(512)}, u32[]{:S(2)}) copy-start(f32[336]{0:T(512)} %param.20) | copy-start | bytes 4036
  107.2 16.5 %copy-start.8 = (f32[336]{0:T(512)S(1)}, f32[336]{0:T(512)}, u32[]{:S(2)}) copy-start(f32[336]{0:T(512)} %param.21) | copy-start | bytes 4036
  109.1 33.9 %all-to-all-start.1 = ((bf16[128,2,960]{2,1,0:T(2,128)(2,1)}), bf16[128,2,960]{2,1,0:T(2,128)(2,1)S(1)}, u32[]{:S(2)}, u32[]{:S(2)}) async-start(bf16[128,2,960]{2,1,0:T(2,128)(2,1)} %reshape.61), calls=%async_computation.1 | async-start | bytes 1048576 | tf_op jit(solution)/shard_map/all_to_all | solution.py:140
  143.7 1.3 copy-start.3
  144.8 1.3 copy-start.4
Sparse Core Ops, SparseCore 0:
  58.3 28.4 all-gather.1
where the time goes:
time: 154 us
  waiting for transfers between devices  53.9 us (35%)
  starting transfers between devices  40.2 us (26%)
  matrix products  18.2 us (12%)
  between operations  15.7 us (10%)
  local copies, waits for them, and re-layouts  13.7 us (9%)
  other arithmetic  12.2 us (8%)
    all_to_all x1, waiting for transfers between devices, per_device(): lax.all_to_all(route_rows(joint_map, joint_pieces), 'shard', split_axis=0...  18.7 us
    all_to_all x1, waiting for transfers between devices, per_device(): lax.all_to_all(own_result.reshape(shards, rows_dev, block_width), 'shard'...  18.6 us
    all_to_all x1, starting transfers between devices, per_device(): lax.all_to_all(route_rows(joint_map, joint_pieces), 'shard', split_axis=0...  18.4 us
    all_gather x1, waiting for transfers between devices, gather_columns(): return lax.all_gather(column_part, 'tensor', axis=1, tiled=True)  16.5 us
    all_to_all x1, starting transfers between devices, per_device(): lax.all_to_all(own_result.reshape(shards, rows_dev, block_width), 'shard'...  14.5 us
    dot_general x4, matrix products, newton_step(): lax.dot_general(full_iterate, polynomial, (((1,), (1,)), ((), ())), prefe...  10.4 us
    unnamed x25, local copies, waits for them, and re-layouts  7.42 us
    all_to_all x1, starting transfers between devices, per_device(): lax.all_to_all(vec_pieces, 'shard', split_axis=0, concat_axis=0, tiled=True)  7.25 us
  transfers between devices with their start and end apart: 4, of which 3 were waited for; matrix products, arithmetic and copies ran while one was open for 17% of the time, Pallas kernels for 0%

commit v1 on v0

--- a/solution.py
+++ b/solution.py
@@ -120,8 +120,16 @@
     matrices = big_grad.shape[0]
     joint_map = owner_table(jnp.concatenate([owners[0], owners[1]]), shards)
     joint_pieces = jnp.concatenate([big_grad, small_grad], axis=0)
-    arrived = lax.all_to_all(
-        route_rows(joint_map, joint_pieces), "shard", split_axis=0, concat_axis=1, tiled=True
+    arrived = jnp.concatenate(
+        lax.all_to_all(
+            jnp.stack(
+                jnp.split(route_rows(joint_map, joint_pieces), lax.axis_size("shard"), axis=0)
+            ),
+            "shard",
+            0,
+            0,
+        ),
+        axis=1,
     )[0]
     big_owner = jnp.any(owners[0] == shard_place)
     small_owner = jnp.any(owners[1] == shard_place)

time: 154 us -> 167 us (1.084)
  local copies, waits for them, and re-layouts: 13.7 us -> 25.6 us
    another operation x0 -> x129, local copies, waits for them, and re-layouts: none -> 11.2 us  [per_device(): jnp.stack(jnp.split(route_rows(joint_map, joint_pieces), lax.axis_size('s...]
    split x0 -> x7, local copies, waits for them, and re-layouts: none -> 2.72 us  [per_device(): jnp.split(route_rows(joint_map, joint_pieces), lax.axis_size('shard'), ax...]
    unnamed x25 -> x152, local copies, waits for them, and re-layouts: 7.42 us -> 7.82 us
  transfers between devices with their start and end apart: 4 -> 4, of which waited for: 3 -> 3; matrix products, arithmetic and copies ran while one was open for 17% -> 16% of each run, Pallas kernels for 0% -> 0%
where the time goes in v1:
time: 167 us
  waiting for transfers between devices  53.7 us (32%)
  starting transfers between devices  40.3 us (24%)
  local copies, waits for them, and re-layouts  25.6 us (15%)
  matrix products  18.2 us (11%)
  between operations  16.8 us (10%)
  other arithmetic  12.2 us (7%)
    all_to_all x1, waiting for transfers between devices, per_device(): lax.all_to_all(own_result.reshape(shards, rows_dev, block_width), 'shard'...  18.6 us
    all_to_all x1, waiting for transfers between devices, per_device(): lax.all_to_all(jnp.stack(jnp.split(route_rows(joint_map, joint_pieces), l...  18.6 us
    all_to_all x1, starting transfers between devices, per_device(): lax.all_to_all(jnp.stack(jnp.split(route_rows(joint_map, joint_pieces), l...  18.4 us
    all_gather x1, waiting for transfers between devices, gather_columns(): return lax.all_gather(column_part, 'tensor', axis=1, tiled=True)  16.6 us
    all_to_all x1, starting transfers between devices, per_device(): lax.all_to_all(own_result.reshape(shards, rows_dev, block_width), 'shard'...  14.5 us
    another operation x129, local copies, waits for them, and re-layouts, per_device(): jnp.stack(jnp.split(route_rows(joint_map, joint_pieces), lax.axis_size('s...  11.2 us
    dot_general x4, matrix products, newton_step(): lax.dot_general(full_iterate, polynomial, (((1,), (1,)), ((), ())), prefe...  10.4 us
    unnamed x152, local copies, waits for them, and re-layouts  7.82 us
  transfers between devices with their start and end apart: 4, of which 3 were waited for; matrix products, arithmetic and copies ran while one was open for 16% of the time, Pallas kernels for 0%

profile of v1, /device:TPU:1, one launch (start us, length us, event | category | flops | bytes accessed | tf_op | source)
XLA Modules:
  0.0 166.8 jit_solution(8958094974873119535)
XLA Ops:
  7.2 1.0 pad_maximum_fusion
  8.2 0.2 copy.296
  8.4 0.4 reshape.295
  8.9 0.3 convolution_convert_fusion
  9.2 0.3 slice_reduce_fusion.114
  9.5 0.4 slice_reduce_fusion.95
  9.9 0.4 slice_reduce_fusion.76
  10.3 0.4 slice_reduce_fusion.57
  10.7 0.4 slice_reduce_fusion.38
  11.1 0.4 slice_reduce_fusion.19
  11.5 0.4 slice_reduce_fusion
  24.6 1.6 reshape.436
  26.1 18.4 %all-to-all-start = ((bf16[128,2,960]{2,1,0:T(2,128)(2,1)}), bf16[128,2,960]{2,1,0:T(2,128)(2,1)S(1)}, u32[]{:S(2)}, u32[]{:S(2)}) async-start(bf16[128,2,960]{2,1,0:T(2,128)(2,1)} %reshape.436), calls=%async_computation | async-start | bytes 1048576 | tf_op jit(solution)/shard_map/all_to_all | solution.py:124
  44.5 0.2 all-gather.2.cloned.1.call-start
  44.8 0.6 compare_reduce_fusion.1
  45.4 18.6 %all-to-all-done = bf16[128,2,960]{2,1,0:T(2,128)(2,1)S(1)} async-done(((bf16[128,2,960]{2,1,0:T(2,128)(2,1)}), bf16[128,2,960]{2,1,0:T(2,128)(2,1)S(1)}, u32[]{:S(2)}, u32[]{:S(2)}) %all-to-all-start) | async-done | bytes 491552 | tf_op jit(solution)/shard_map/all_to_all | solution.py:124
  64.0 0.8 reshape.437
  64.7 0.4 reshape.298
  65.1 0.4 copy.297
  65.5 0.8 copy-done.1
  66.3 4.9 %fusion.17 = (f32[1,192,1280]{2,1,0:T(8,128)}, bf16[1280,192]{0,1:T(8,128)(2,1)}, f32[1,192,1280]{2,1,0:T(8,128)}, f32[]{:T(128)}, bf16[192,1280]{1,0:T(8,128)(2,1)S(1)}) fusion(f32[1,192,1280]{2,1,0:T(8,128)S(1)} %copy-done.1, f32[1280,192]{0,1:T(8,128)S(1)} %copy.297, pred[]{:T(512)} %get-tuple-element.156, f32[1,192,1280]{2,1,0:T(8,128)} %param.16, ...), kind=kLoop, calls=%fused_computation.39 | loop fusion | flops 4177919 | bytes 5898246 | tf_op jit(solution)/shard_map/broadcast_in_dim | solution.py:169
  71.2 0.5 broadcast.199
  71.7 1.0 reduce.261
  72.8 1.0 all_to_all.16
  73.8 7.2 %all-to-all-start.2 = ((f32[128,1,336]{2,1,0:T(1,128)}), f32[128,1,336]{2,1,0:T(1,128)S(1)}, u32[]{:S(2)}, u32[]{:S(2)}) async-start(f32[128,1,336]{2,1,0:T(1,128)} %all_to_all.16), calls=%async_computation.2 | async-start | bytes 393216 | tf_op jit(solution)/shard_map/all_to_all | solution.py:160
  81.7 0.3 convolution_convert_fusion.5
  82.1 0.4 fusion.3
  82.5 0.3 convolution_convert_fusion.4
  82.8 0.4 fusion.4
  83.3 16.6 %all-gather.2.cloned.1.call-done = bf16[1280,768]{0,1:T(8,128)(2,1)} async-done(((bf16[1280,192]{0,1:T(8,128)(2,1)}), bf16[1280,768]{0,1:T(8,128)(2,1)}) %all-gather.2.cloned.1.call-update) | async-done | bytes 1966096 | tf_op jit(solution)/shard_map/all_gather | solution.py:95
  99.8 3.3 %fusion = f32[]{:T(128)} fusion(bf16[1280,768]{0,1:T(8,128)(2,1)} %all-gather.2.cloned.1.call-done), kind=kLoop, calls=%fused_computation.2 | loop fusion | flops 2949119 | bytes 1966084 | tf_op jit(solution)/shard_map/reduce_sum | solution.py:53
  103.8 2.8 %convolution_convert_fusion.3 = bf16[768,768]{1,0:T(8,128)(2,1)} fusion(bf16[1280,768]{0,1:T(8,128)(2,1)S(1)} %copy-done, f32[]{:T(128)S(6)} %add.66), kind=kOutput, calls=%fused_computation.16 | convolution fusion | flops 1513488384 | bytes 3145732 | tf_op jit(solution)/shard_map/dot_general | solution.py:58
  106.6 6.3 %add_convert_fusion = bf16[1280,768]{0,1:T(8,128)(2,1)} fusion(bf16[768,768]{1,0:T(8,128)(2,1)} %convolution_convert_fusion.3, f32[]{:T(128)S(6)} %add.66, bf16[1280,768]{0,1:T(8,128)(2,1)S(1)} %copy-done), kind=kOutput, calls=%fused_computation.4 | convolution fusion | flops 2428698624 | bytes 5111812 | tf_op jit(solution)/shard_map/dot_general | solution.py:72
  112.9 3.8 %convolution_convert_fusion.2 = bf16[768,768]{1,0:T(8,128)(2,1)S(1)} fusion(bf16[1280,768]{0,1:T(8,128)(2,1)} %add_convert_fusion), kind=kOutput, calls=%fused_computation.15 | convolution fusion | flops 1510539264 | bytes 3145728 | tf_op jit(solution)/shard_map/dot_general | solution.py:58
  116.7 3.2 %fusion.5 = bf16[1280,192]{0,1:T(8,128)(2,1)S(1)} fusion(bf16[1280,192]{0,1:T(8,128)(2,1)S(1)} %fusion.4, bf16[1280,768]{0,1:T(8,128)(2,1)} %add_convert_fusion, bf16[768,768]{1,0:T(8,128)(2,1)S(1)} %convolution_convert_fusion.2, s32[]{:T(128)S(6)} %select_n.39, pred[]{:T(512)} %get-tuple-element.156), kind=kOutput, calls=%fused_computation.11 | convolution fusion | flops 605945856 | bytes 5212160 | tf_op jit(solution)/shard_map/dot_general | solution.py:72
  119.9 0.2 copy.298
  120.2 0.3 reshape.296
  120.5 1.6 reshape.438
  122.1 14.5 %all-to-all-start.1 = ((bf16[128,2,960]{2,1,0:T(2,128)(2,1)}), bf16[128,2,960]{2,1,0:T(2,128)(2,1)S(1)}, u32[]{:S(2)}, u32[]{:S(2)}) async-start(bf16[128,2,960]{2,1,0:T(2,128)(2,1)} %reshape.438), calls=%async_computation.1 | async-start | bytes 1048576 | tf_op jit(solution)/shard_map/all_to_all | solution.py:148
  136.5 0.2 reduce_sum.29
  136.7 0.6 divide_subtract_fusion
  137.3 18.6 %all-to-all-done.1 = bf16[128,2,960]{2,1,0:T(2,128)(2,1)S(1)} async-done(((bf16[128,2,960]{2,1,0:T(2,128)(2,1)}), bf16[128,2,960]{2,1,0:T(2,128)(2,1)S(1)}, u32[]{:S(2)}, u32[]{:S(2)}) %all-to-all-start.1) | async-done | bytes 491552 | tf_op jit(solution)/shard_map/all_to_all | solution.py:148
  155.9 0.8 reshape.439
  156.7 0.7 copy.299
  157.5 0.3 convolution_convert_fusion.1
  158.0 0.2 fusion.26
  158.2 0.7 copy.302
  159.3 0.7 copy.303
  (281 shorter events, 12.3 us)
Async XLA Ops:
  7.2 1.6 copy-start.5
  26.1 37.8 %all-to-all-start = ((bf16[128,2,960]{2,1,0:T(2,128)(2,1)}), bf16[128,2,960]{2,1,0:T(2,128)(2,1)S(1)}, u32[]{:S(2)}, u32[]{:S(2)}) async-start(bf16[128,2,960]{2,1,0:T(2,128)(2,1)} %reshape.436), calls=%async_computation | async-start | bytes 1048576 | tf_op jit(solution)/shard_map/all_to_all | solution.py:124
  44.5 55.3 %all-gather.2.cloned.1.call-start = ((), (), s32[]{:S(2)}) async-start(), calls=%async_computation.3 | async-start | bytes 2457600 | tf_op jit(solution)/shard_map/all_gather | solution.py:95
  65.1 1.2 copy-start.1
  66.3 5.4 %copy-start.2 = (f32[1,43008]{1,0:T(1,128)S(1)}, f32[1,43008]{1,0:T(1,128)}, u32[]{:S(2)}) copy-start(f32[1,43008]{1,0:T(1,128)} %param.18) | copy-start | bytes 516100
  73.8 48.3 %all-to-all-start.2 = ((f32[128,1,336]{2,1,0:T(1,128)}), f32[128,1,336]{2,1,0:T(1,128)S(1)}, u32[]{:S(2)}, u32[]{:S(2)}) async-start(f32[128,1,336]{2,1,0:T(1,128)} %all_to_all.16), calls=%async_computation.2 | async-start | bytes 393216 | tf_op jit(solution)/shard_map/all_to_all | solution.py:160
  99.8 4.0 %copy-start = (bf16[1280,768]{0,1:T(8,128)(2,1)S(1)}, bf16[1280,768]{0,1:T(8,128)(2,1)}, u32[]{:S(2)}) copy-start(bf16[1280,768]{0,1:T(8,128)(2,1)} %all-gather.2.cloned.1.call-done) | copy-start | bytes 5898244
  120.2 16.5 %copy-start.6 = (f32[336]{0:T(512)S(1)}, f32[336]{0:T(512)}, u32[]{:S(2)}) copy-start(f32[336]{0:T(512)} %param.19) | copy-start | bytes 4036
  120.2 16.5 %copy-start.7 = (f32[336]{0:T(512)S(1)}, f32[336]{0:T(512)}, u32[]{:S(2)}) copy-start(f32[336]{0:T(512)} %param.20) | copy-start | bytes 4036
  120.2 16.5 %copy-start.8 = (f32[336]{0:T(512)S(1)}, f32[336]{0:T(512)}, u32[]{:S(2)}) copy-start(f32[336]{0:T(512)} %param.21) | copy-start | bytes 4036
  122.1 33.9 %all-to-all-start.1 = ((bf16[128,2,960]{2,1,0:T(2,128)(2,1)}), bf16[128,2,960]{2,1,0:T(2,128)(2,1)S(1)}, u32[]{:S(2)}, u32[]{:S(2)}) async-start(bf16[128,2,960]{2,1,0:T(2,128)(2,1)} %reshape.438), calls=%async_computation.1 | async-start | bytes 1048576 | tf_op jit(solution)/shard_map/all_to_all | solution.py:148
  156.7 1.3 copy-start.3
  157.8 1.3 copy-start.4
Sparse Core Ops, SparseCore 0:
  71.3 28.4 all-gather.1
